TPU v7x, 512 devices: a whole 4x8x8 slice. The times are simulated.
512 devices in a mesh: section: 4 (over x_lo, core), batch: 128 (over z, y, x_hi).
Axes of the slice: x: 4 (x_hi: 2, x_lo: 2; x = x_hi * 2 + x_lo), y: 8, z: 8, core: 2. Of those that a mesh axis runs over, the one named last changes fastest.
Arguments:
- latents: bfloat16 [4096, 512], P('batch'), may hold values from -6 to 6
- token_slot: int32 [4096], P('batch'), may hold values from 0 to 4095, as said below
- cache_keys: bfloat16 [4096, 128, 512], P('batch', None, 'section'), may hold values from -320 to 320
- cache_values: bfloat16 [4096, 128, 512], P('batch', None, 'section'), may hold values from -6 to 6
- up_state: bfloat16 [4096, 512], P('batch'), may hold values from -6 to 6
- conv_state: bfloat16 [4096, 512], P('batch'), may hold values from -1 to 3
- cache_slot: int32 [4096], P('batch'), may hold values from 0 to 4095, as said below
- positions: int32 [4096], P('batch'), may hold values from 0 to 512
- up_kernel: float32 [4, 512], replicated, may hold values from -4 to 4
- norm_gain_one: float32 [512], replicated, may hold values from 0.1 to 1.9
- qkv_weight: bfloat16 [3, 512, 512], P(None, None, 'section'), may hold values from -0.25 to 0.25
- out_weight: bfloat16 [512, 512], P('section'), may hold values from -0.25 to 0.25
- scale_attention: float32 [512], replicated, may hold values from 0.1 to 1.9
- norm_gain_two: float32 [512], replicated, may hold values from 0.1 to 1.9
- in_weight: bfloat16 [512, 2048], P(None, 'section'), may hold values from -0.25 to 0.25
- down_weight: bfloat16 [2048, 512], P('section'), may hold values from -0.125 to 0.125
- scale_feedforward: float32 [512], replicated, may hold values from 0.1 to 1.9
- conv_weight: bfloat16 [16, 256, 512], P(None, 'section'), may hold values from -0.1875 to 0.1875
- conv_bias: float32 [256], P('section'), may hold values from -3 to 3
Outputs:
- audio_out: float32 [256, 65536], P('section', 'batch')
- new_keys: bfloat16 [4096, 128, 512], P('batch', None, 'section')
- new_values: bfloat16 [4096, 128, 512], P('batch', None, 'section')
- new_up_state: bfloat16 [4096, 512], P('batch')
- new_conv_state: bfloat16 [4096, 512], P('batch')
Inputs may be any that keep to these rules, and one draw needn't show every extreme that they name: `token_slot`: every slot receives exactly one token row. The 32 rows of one transformer owner go in groups of exactly 2 rows to 16 different decoder owners; the decoder owner of slot n is n // 32. `cache_slot`: A permutation of the slots. Each batch index keeps all but 2 * 1 of its streams and hands exactly 1 to the index one higher and 1 to the index one lower, cyclically.
All inputs are finite; a program needn't handle non-finite values.
Results may differ from a plain program's by a relative error of at most 0.017.
Values may be sent and summed in bfloat16 or wider, within the bound.
No kernel may reach another device: no remote copies, remote signals or barrier semaphores. Data moves between devices by JAX's collectives and lax.ppermute only.
A program may use at most 64 MiB of HBM per device.

v0:
```python
import jax
import jax.numpy as jnp
from jax import lax
from jax.sharding import PartitionSpec as P

HEAD_DIM = 64
MOVE = 1
EPSILON = 1e-05
MAX_PERIOD = 10000.0


def for_sending(array):

    def short(part):
        return part.astype(jnp.bfloat16) if part.dtype == jnp.float32 else part

    return jax.tree.map(short, array)


def passed_along(block, axis, distance):
    devices = range(lax.axis_size(axis))
    route = [((i - distance) % len(devices), i) for i in devices]
    return lax.ppermute(block, axis, route)


def layer_norm(hidden, weight_gain):
    average = jnp.mean(hidden, axis=-1, keepdims=True)
    centred = hidden - average
    variance = jnp.mean(centred * centred, axis=-1, keepdims=True)
    return centred * lax.rsqrt(variance + EPSILON) * weight_gain


def rotate(features, times, head_width):
    streams = features.shape[0]
    half = head_width // 2
    freqs = MAX_PERIOD ** (-2.0 * jnp.arange(half, dtype=jnp.float32) / head_width)
    angle = times.astype(jnp.float32)[:, :, None] * freqs[None, None, :]
    cosine = jnp.cos(angle)[:, :, None, :]
    sine = jnp.sin(angle)[:, :, None, :]
    paired = features.reshape(streams, 2, -1, half, 2)
    first = paired[..., 0]
    second = paired[..., 1]
    turned = jnp.stack([first * cosine - second * sine, first * sine + second * cosine], axis=-1)
    return turned.reshape(features.shape)


def attend(
    queries, fresh_keys, fresh_values, old_keys, old_values, starts, local_heads, head_width
):
    streams = old_keys.shape[0]
    window = old_keys.shape[1]
    query_heads = queries.reshape(streams, 2, local_heads, head_width)
    cache_heads = old_keys.reshape(streams, window, local_heads, head_width)
    fresh_heads = fresh_keys.reshape(streams, 2, local_heads, head_width)
    score_scale = head_width ** (-0.5)
    cache_scores = (
        jnp.einsum("sfhe,swhe->shfw", query_heads, cache_heads, preferred_element_type=jnp.float32)
        * score_scale
    )
    fresh_scores = (
        jnp.einsum("sfhe,sghe->shfg", query_heads, fresh_heads, preferred_element_type=jnp.float32)
        * score_scale
    )
    cycle_slots = jnp.arange(window, dtype=jnp.int32)
    held_time = starts[:, None] - window + jnp.mod(cycle_slots[None, :] - starts[:, None], window)
    query_times = starts[:, None] + jnp.arange(2, dtype=jnp.int32)[None, :]
    cache_ok = (held_time[:, None, :] >= 0) & (
        held_time[:, None, :] > query_times[:, :, None] - window
    )
    frame_ids = jnp.arange(2, dtype=jnp.int32)
    fresh_ok = frame_ids[None, :] <= frame_ids[:, None]
    allowed = jnp.concatenate(
        [
            jnp.broadcast_to(cache_ok[:, None], (streams, local_heads, 2, window)),
            jnp.broadcast_to(fresh_ok, (streams, local_heads, 2, 2)),
        ],
        axis=-1,
    )
    scores = jnp.concatenate([cache_scores, fresh_scores], axis=-1)
    scores = jnp.where(allowed, scores, -jnp.inf)
    score_max = jnp.max(scores, axis=-1, keepdims=True)
    weights = jnp.where(allowed, jnp.exp(scores - score_max), 0.0)
    denominator = jnp.sum(weights, axis=-1, keepdims=True)
    rounded = weights.astype(jnp.bfloat16)
    value_heads = old_values.reshape(streams, window, local_heads, head_width)
    fresh_value_heads = fresh_values.reshape(streams, 2, local_heads, head_width)
    attended = jnp.einsum(
        "shfw,swhe->sfhe", rounded[..., :window], value_heads, preferred_element_type=jnp.float32
    )
    attended = attended + jnp.einsum(
        "shfg,sghe->sfhe",
        rounded[..., window:],
        fresh_value_heads,
        preferred_element_type=jnp.float32,
    )
    attended = attended / jnp.transpose(denominator, (0, 2, 1, 3))
    return attended.astype(jnp.bfloat16).reshape(streams, 2, local_heads * head_width)


def pack_side(direction_owner, leaving, dest_owner, slot_ids, outgoing):
    chosen = leaving & (dest_owner == direction_owner)
    before = chosen[None, :] & (slot_ids[None, :] < slot_ids[:, None])
    box_place = jnp.where(chosen, jnp.sum(before.astype(jnp.int32), axis=1), MOVE)
    return tuple(
        (
            jnp.zeros((MOVE,) + source_array.shape[1:], source_array.dtype)
            .at[box_place]
            .set(source_array, mode="drop")
            for source_array in outgoing
        )
    )


def local(
    latents,
    token_slot,
    cache_keys,
    cache_values,
    up_state,
    conv_state,
    cache_slot,
    positions,
    up_kernel,
    norm_gain_one,
    qkv_weight,
    out_weight,
    scale_attention,
    norm_gain_two,
    in_weight,
    down_weight,
    scale_feedforward,
    conv_weight,
    conv_bias,
):
    owners = lax.axis_size("batch")
    own_index = lax.axis_index("batch")
    streams = latents.shape[0]
    model_width = latents.shape[1]
    window = cache_keys.shape[1]
    head_share = cache_keys.shape[2]
    capacity = max(2, streams // owners)
    slot_ids = jnp.arange(streams, dtype=jnp.int32)
    target = token_slot // streams
    landing = token_slot % streams
    same_before = (target[None, :] == target[:, None]) & (slot_ids[None, :] < slot_ids[:, None])
    arrival_rank = jnp.sum(same_before.astype(jnp.int32), axis=1)
    send_rows = (
        jnp.zeros((owners, capacity, model_width), jnp.bfloat16)
        .at[target, arrival_rank]
        .set(latents)
    )
    send_codes = (
        jnp.zeros((owners, capacity), jnp.bfloat16)
        .at[target, arrival_rank]
        .set((landing + 1).astype(jnp.bfloat16))
    )
    got_rows, got_codes = (
        lax.all_to_all(send_rows, "batch", split_axis=0, concat_axis=0, tiled=True),
        lax.all_to_all(send_codes, "batch", split_axis=0, concat_axis=0, tiled=True),
    )
    selector = got_codes.reshape(-1).astype(jnp.int32)[None, :] - 1 == slot_ids[:, None]
    arrived = jnp.dot(
        selector.astype(jnp.bfloat16),
        got_rows.reshape(owners * capacity, model_width),
        preferred_element_type=jnp.float32,
    ).astype(jnp.bfloat16)
    dest_owner = cache_slot // streams
    dest_local = cache_slot % streams
    leaving = dest_owner != own_index
    stay_codes = jnp.where(leaving, 0, dest_local + 1).astype(jnp.bfloat16)
    code_values = (dest_local + 1).astype(jnp.bfloat16)
    outgoing = (cache_keys, cache_values, up_state, conv_state, code_values)
    right_owner = jnp.mod(own_index + 1, owners)
    left_owner = jnp.mod(own_index + owners - 1, owners)
    right_parts = pack_side(right_owner, leaving, dest_owner, slot_ids, outgoing)
    left_parts = pack_side(left_owner, leaving, dest_owner, slot_ids, outgoing)
    from_left = jax.tree.map(
        lambda part, own: part.astype(own.dtype),
        passed_along(for_sending(right_parts), "batch", 1),
        right_parts,
    )
    from_right = jax.tree.map(
        lambda part, own: part.astype(own.dtype),
        passed_along(for_sending(left_parts), "batch", -1),
        left_parts,
    )
    incoming = tuple(
        (
            jnp.concatenate([lower_part, upper_part], axis=0)
            for lower_part, upper_part in zip(from_left, from_right)
        )
    )
    candidate = tuple(
        (
            jnp.concatenate([own_array, extra_array], axis=0)
            for own_array, extra_array in zip(
                (cache_keys, cache_values, up_state, conv_state, stay_codes), incoming
            )
        )
    )
    candidate_codes = candidate[4].astype(jnp.int32) - 1
    matches = candidate_codes[None, :] == slot_ids[:, None]
    picked = jnp.sum(
        jnp.where(matches, jnp.arange(candidate_codes.shape[0], dtype=jnp.int32)[None, :], 0),
        axis=1,
    )
    keys_old = jnp.take(candidate[0], picked, axis=0)
    values_old = jnp.take(candidate[1], picked, axis=0)
    up_prev = jnp.take(candidate[2], picked, axis=0)
    conv_prev = jnp.take(candidate[3], picked, axis=0)
    latent_f = arrived.astype(jnp.float32)
    prior_f = up_prev.astype(jnp.float32)
    residual_zero = jnp.stack(
        [
            latent_f * up_kernel[0] + prior_f * up_kernel[2],
            latent_f * up_kernel[1] + prior_f * up_kernel[3],
        ],
        axis=1,
    )
    normed_one = layer_norm(residual_zero, norm_gain_one).astype(jnp.bfloat16)
    projections = jnp.einsum(
        "sfd,kde->ksfe", normed_one, qkv_weight, preferred_element_type=jnp.float32
    )
    times = positions[:, None] + jnp.arange(2, dtype=jnp.int32)[None, :]
    queries = rotate(projections[0], times, HEAD_DIM).astype(jnp.bfloat16)
    fresh_keys = rotate(projections[1], times, HEAD_DIM).astype(jnp.bfloat16)
    fresh_values = projections[2].astype(jnp.bfloat16)
    attended = attend(
        queries,
        fresh_keys,
        fresh_values,
        keys_old,
        values_old,
        positions,
        head_share // HEAD_DIM,
        HEAD_DIM,
    )
    partial_heads = jnp.dot(
        attended.reshape(2 * streams, head_share), out_weight, preferred_element_type=jnp.float32
    )
    mixing = lax.psum(partial_heads.astype(jnp.bfloat16), "section").astype(jnp.float32)
    residual_one = residual_zero + scale_attention * mixing.reshape(streams, 2, model_width)
    normed_two = (
        layer_norm(residual_one, norm_gain_two)
        .astype(jnp.bfloat16)
        .reshape(2 * streams, model_width)
    )
    inner_units = jax.nn.gelu(
        jnp.dot(normed_two, in_weight, preferred_element_type=jnp.float32), approximate=False
    ).astype(jnp.bfloat16)
    partial_units = jnp.dot(inner_units, down_weight, preferred_element_type=jnp.float32)
    feed_forward = lax.psum(partial_units.astype(jnp.bfloat16), "section").astype(jnp.float32)
    residual_two = residual_one + scale_feedforward * feed_forward.reshape(streams, 2, model_width)
    excited = jax.nn.elu(residual_two).astype(jnp.bfloat16)
    earlier = jnp.stack([conv_prev, excited[:, 0]], axis=1)
    stride = conv_weight.shape[0] // 2
    audio_out = jnp.einsum(
        "sfi,rci->csfr", excited, conv_weight[:stride], preferred_element_type=jnp.float32
    )
    audio_out = audio_out + jnp.einsum(
        "sfi,rci->csfr", earlier, conv_weight[stride:], preferred_element_type=jnp.float32
    )
    audio_out = audio_out + conv_bias[:, None, None, None]
    audio_out = audio_out.reshape(conv_bias.shape[0], streams * 2 * stride)
    slot_first = jnp.mod(positions, window)
    slot_second = jnp.mod(positions + 1, window)
    new_keys = (
        keys_old.at[slot_ids, slot_first]
        .set(fresh_keys[:, 0])
        .at[slot_ids, slot_second]
        .set(fresh_keys[:, 1])
    )
    new_values = (
        values_old.at[slot_ids, slot_first]
        .set(fresh_values[:, 0])
        .at[slot_ids, slot_second]
        .set(fresh_values[:, 1])
    )
    return (audio_out, new_keys, new_values, arrived, excited[:, 1])


def solution(mesh):
    placed = (
        P("batch", None),
        P("batch"),
        P("batch", None, "section"),
        P("batch", None, "section"),
        P("batch", None),
        P("batch", None),
        P("batch"),
        P("batch"),
        P(),
        P(),
        P(None, None, "section"),
        P("section", None),
        P(),
        P(),
        P(None, "section"),
        P("section", None),
        P(),
        P(None, "section", None),
        P("section"),
    )
    return jax.shard_map(
        local,
        mesh=mesh,
        in_specs=placed,
        out_specs=(
            P("section", "batch"),
            P("batch", None, "section"),
            P("batch", None, "section"),
            P("batch", None),
            P("batch", None),
        ),
        check_vma=False,
    )
```

profile of v0, /device:TPU:1, one launch (start us, length us, event | category | flops | bytes accessed | tf_op | source)
XLA Modules:
  0.0 243.5 jit_solution(4903698463168684158)
XLA Ops:
  8.1 2.0 scatter_fusion
  10.9 20.8 %all-to-all-start = ((bf16[128,1,2]{2,1,0:T(2,128)(2,1)}), bf16[128,1,2]{2,1,0:T(2,128)(2,1)S(1)}, u32[]{:S(2)}, u32[]{:S(2)}) async-start(bf16[128,1,2]{2,1,0:T(2,128)(2,1)} %copy.94), calls=%async_computation | async-start | bytes 131072 | tf_op jit(solution)/shard_map/all_to_all | solution.py:159
  32.7 9.0 %collective-permute-start.1 = (bf16[1,512]{1,0:T(2,128)(2,1)S(1)}, bf16[1,512]{1,0:T(2,128)(2,1)S(1)}, u32[]{:S(2)}, u32[]{:S(2)}) collective-permute-start(bf16[1,512]{1,0:T(2,128)(2,1)S(1)} %bitcast.138), channel_id=1, source_target_pairs={{1,0},{2,1},{3,2},{4,3},{5,4},{6,5},{7,6},{8,7},{9,8},{10,9},{11,1... | collective-permute-start | bytes 3080 | tf_op jit(solution)/shard_map/ppermute | solution.py:23
  42.5 1.9 collective-permute-start
  46.2 9.1 %collective-permute-start.3 = (bf16[1]{0:T(256)(128)(2,1)}, bf16[1]{0:T(256)(128)(2,1)}, u32[]{:S(2)}, u32[]{:S(2)}) collective-permute-start(bf16[1]{0:T(256)(128)(2,1)} %scatter_fusion.3), channel_id=1, source_target_pairs={{1,0},{2,1},{3,2},{4,3},{5,4},{6,5},{7,6},{8,7},{9,8},{10,9},{11,1... | collective-permute-start | bytes 14 | tf_op jit(solution)/shard_map/ppermute | solution.py:23
  55.3 1.8 scatter_fusion.2
  57.0 1.9 collective-permute-start.2
  60.7 9.1 %collective-permute-start.5 = (bf16[1,128,128]{2,1,0:T(8,128)(2,1)S(1)}, bf16[1,128,128]{2,1,0:T(8,128)(2,1)S(1)}, u32[]{:S(2)}, u32[]{:S(2)}) collective-permute-start(bf16[1,128,128]{2,1,0:T(8,128)(2,1)S(1)} %bitcast.120), channel_id=1, source_target_pairs={{1,0},{2,1},{3,2},{4,3},{5,4},{6,5},{7,6},{8,7},{9,8},{10,9},{11,1... | collective-permute-start | bytes 98312 | tf_op jit(solution)/shard_map/ppermute | solution.py:23
  77.6 4.4 %scatter_fusion.1 = bf16[128,2,512]{2,1,0:T(2,128)(2,1)} fusion(bf16[128,2,512]{2,1,0:T(2,128)(2,1)} %broadcast_in_dim.65, s32[32]{0:T(128)S(1)} %fusion.115, bf16[32,512]{1,0:T(8,128)(2,1)S(1)} %copy-done.10), kind=kCustom, calls=%fused_computation.5 | custom fusion | bytes 98560 | tf_op jit(solution)/shard_map/scatter | solution.py:150
  82.4 1.9 collective-permute-start.9
  84.3 4.9 %collective-permute-start.8 = (bf16[1,512]{1,0:T(2,128)(2,1)S(1)}, bf16[1,512]{1,0:T(2,128)(2,1)S(1)}, u32[]{:S(2)}, u32[]{:S(2)}) collective-permute-start(bf16[1,512]{1,0:T(2,128)(2,1)S(1)} %bitcast.140), channel_id=1, source_target_pairs={{127,0},{0,1},{1,2},{2,3},{3,4},{4,5},{5,6},{6,7},{7,8},{8,9},{9,1... | collective-permute-start | bytes 3080 | tf_op jit(solution)/shard_map/ppermute | solution.py:23
  90.7 7.8 %all-to-all-start.1 = ((bf16[128,2,512]{2,1,0:T(2,128)(2,1)}), bf16[128,2,512]{2,1,0:T(2,128)(2,1)S(1)}, u32[]{:S(2)}, u32[]{:S(2)}) async-start(bf16[128,2,512]{2,1,0:T(2,128)(2,1)} %scatter_fusion.1), calls=%async_computation.1 | async-start | bytes 524288 | tf_op jit(solution)/shard_map/all_to_all | solution.py:158
  99.0 4.0 %collective-permute-start.4 = (bf16[1,128,128]{2,1,0:T(8,128)(2,1)S(1)}, bf16[1,128,128]{2,1,0:T(8,128)(2,1)S(1)}, u32[]{:S(2)}, u32[]{:S(2)}) collective-permute-start(bf16[1,128,128]{2,1,0:T(8,128)(2,1)S(1)} %bitcast.121), channel_id=1, source_target_pairs={{127,0},{0,1},{1,2},{2,3},{3,4},{4,5},{5,6},{6,7},{7,8},{8,9},{9,1... | collective-permute-start | bytes 98312 | tf_op jit(solution)/shard_map/ppermute | solution.py:23
  103.0 7.0 %collective-permute-start.7 = (bf16[1,128,128]{2,1,0:T(8,128)(2,1)S(1)}, bf16[1,128,128]{2,1,0:T(8,128)(2,1)S(1)}, u32[]{:S(2)}, u32[]{:S(2)}) collective-permute-start(bf16[1,128,128]{2,1,0:T(8,128)(2,1)S(1)} %bitcast.122), channel_id=1, source_target_pairs={{1,0},{2,1},{3,2},{4,3},{5,4},{6,5},{7,6},{8,7},{9,8},{10,9},{11,1... | collective-permute-start | bytes 98312 | tf_op jit(solution)/shard_map/ppermute | solution.py:23
  110.7 2.1 collective-permute-start.6
  114.7 2.9 %gather_fusion.1 = bf16[32,128,128]{2,1,0:T(8,128)(2,1)} fusion(bf16[34,128,128]{2,1,0:T(8,128)(2,1)} %pad_maximum_fusion, s32[1024]{0:T(1024)S(1)} %pad_clamp_fusion), kind=kCustom, calls=%fused_computation.1.clone | custom fusion | bytes 2097280 | tf_op jit(solution)/shard_map/jit(_take)/gather | solution.py:208
  117.6 3.6 %collective-permute-done.6 = bf16[1,128,128]{2,1,0:T(8,128)(2,1)S(1)} collective-permute-done((bf16[1,128,128]{2,1,0:T(8,128)(2,1)S(1)}, bf16[1,128,128]{2,1,0:T(8,128)(2,1)S(1)}, u32[]{:S(2)}, u32[]{:S(2)}) %collective-permute-start.6) | collective-permute-done | bytes 32800 | tf_op jit(solution)/shard_map/ppermute | solution.py:23
  122.9 1.8 broadcast_select_fusion.1
  135.7 44.9 %all-reduce.3.cloned.1.call-done = bf16[64,512]{1,0:T(8,128)(2,1)} async-done(((bf16[64,512]{1,0:T(8,128)(2,1)}), bf16[64,512]{1,0:T(8,128)(2,1)}) %all-reduce.3.cloned.1.call-update) | async-done | bytes 65552 | tf_op jit(solution)/shard_map/psum | solution.py:241
  185.3 2.1 scatter_fusion.8
  187.4 2.1 scatter_fusion.10
  189.6 2.1 scatter_fusion.9
  191.7 2.1 scatter_fusion.11
  193.9 38.3 %all-reduce.5.cloned.1.call-done = bf16[32,2,512]{2,0,1:T(8,128)(2,1)} async-done(((bf16[32,2,512]{2,0,1:T(8,128)(2,1)}), bf16[32,2,512]{2,0,1:T(8,128)(2,1)}) %all-reduce.5.cloned.1.call-update) | async-done | bytes 65552 | tf_op jit(solution)/shard_map/psum | solution.py:252
  (164 shorter events, 40.9 us)
Async XLA Ops:
  7.2 175.4 %copy-start = (bf16[512,512]{1,0:T(8,128)(2,1)S(1)}, bf16[512,512]{1,0:T(8,128)(2,1)}, u32[]{:S(2)}) copy-start(bf16[512,512]{1,0:T(8,128)(2,1)} %param.38) | copy-start | bytes 1572868
  7.2 24.6 %copy-start.19 = (s32[32]{0:T(128)S(1)}, s32[32]{0:T(128)}, u32[]{:S(2)}) copy-start(s32[32]{0:T(128)} %param.29) | copy-start | bytes 388
  7.2 24.8 %copy-start.12 = (bf16[32,512]{1,0:T(8,128)(2,1)S(1)}, bf16[32,512]{1,0:T(8,128)(2,1)}, u32[]{:S(2)}) copy-start(bf16[32,512]{1,0:T(8,128)(2,1)} %param.27) | copy-start | bytes 98308
  10.9 79.8 %all-to-all-start = ((bf16[128,1,2]{2,1,0:T(2,128)(2,1)}), bf16[128,1,2]{2,1,0:T(2,128)(2,1)S(1)}, u32[]{:S(2)}, u32[]{:S(2)}) async-start(bf16[128,1,2]{2,1,0:T(2,128)(2,1)} %copy.94), calls=%async_computation | async-start | bytes 131072 | tf_op jit(solution)/shard_map/all_to_all | solution.py:159
  31.8 27.2 %copy-start.1 = (bf16[32,128,128]{2,1,0:T(8,128)(2,1)S(1)}, bf16[32,128,128]{2,1,0:T(8,128)(2,1)}, u32[]{:S(2)}) copy-start(bf16[32,128,128]{2,1,0:T(8,128)(2,1)} %param.26) | copy-start | bytes 3145732
  32.7 78.0 %collective-permute-start.1 = (bf16[1,512]{1,0:T(2,128)(2,1)S(1)}, bf16[1,512]{1,0:T(2,128)(2,1)S(1)}, u32[]{:S(2)}, u32[]{:S(2)}) collective-permute-start(bf16[1,512]{1,0:T(2,128)(2,1)S(1)} %bitcast.138), channel_id=1, source_target_pairs={{1,0},{2,1},{3,2},{4,3},{5,4},{6,5},{7,6},{8,7},{9,8},{10,9},{11,1... | collective-permute-start | bytes 3080 | tf_op jit(solution)/shard_map/ppermute | solution.py:23
  42.5 70.4 %collective-permute-start = (bf16[1,512]{1,0:T(2,128)(2,1)S(1)}, bf16[1,512]{1,0:T(2,128)(2,1)S(1)}, u32[]{:S(2)}, u32[]{:S(2)}) collective-permute-start(bf16[1,512]{1,0:T(2,128)(2,1)S(1)} %bitcast.139), channel_id=1, source_target_pairs={{127,0},{0,1},{1,2},{2,3},{3,4},{4,5},{5,6},{6,7},{7,8},{8,9},{9,1... | collective-permute-start | bytes 3080 | tf_op jit(solution)/shard_map/ppermute | solution.py:23
  46.2 38.1 %collective-permute-start.3 = (bf16[1]{0:T(256)(128)(2,1)}, bf16[1]{0:T(256)(128)(2,1)}, u32[]{:S(2)}, u32[]{:S(2)}) collective-permute-start(bf16[1]{0:T(256)(128)(2,1)} %scatter_fusion.3), channel_id=1, source_target_pairs={{1,0},{2,1},{3,2},{4,3},{5,4},{6,5},{7,6},{8,7},{9,8},{10,9},{11,1... | collective-permute-start | bytes 14 | tf_op jit(solution)/shard_map/ppermute | solution.py:23
  57.0 25.3 %collective-permute-start.2 = (bf16[1]{0:T(256)(128)(2,1)}, bf16[1]{0:T(256)(128)(2,1)}, u32[]{:S(2)}, u32[]{:S(2)}) collective-permute-start(bf16[1]{0:T(256)(128)(2,1)} %scatter_fusion.2), channel_id=1, source_target_pairs={{127,0},{0,1},{1,2},{2,3},{3,4},{4,5},{5,6},{6,7},{7,8},{8,9},{9,1... | collective-permute-start | bytes 14 | tf_op jit(solution)/shard_map/ppermute | solution.py:23
  60.7 52.8 %collective-permute-start.5 = (bf16[1,128,128]{2,1,0:T(8,128)(2,1)S(1)}, bf16[1,128,128]{2,1,0:T(8,128)(2,1)S(1)}, u32[]{:S(2)}, u32[]{:S(2)}) collective-permute-start(bf16[1,128,128]{2,1,0:T(8,128)(2,1)S(1)} %bitcast.120), channel_id=1, source_target_pairs={{1,0},{2,1},{3,2},{4,3},{5,4},{6,5},{7,6},{8,7},{9,8},{10,9},{11,1... | collective-permute-start | bytes 98312 | tf_op jit(solution)/shard_map/ppermute | solution.py:23
  82.4 16.6 %collective-permute-start.9 = (bf16[1,512]{1,0:T(2,128)(2,1)S(1)}, bf16[1,512]{1,0:T(2,128)(2,1)S(1)}, u32[]{:S(2)}, u32[]{:S(2)}) collective-permute-start(bf16[1,512]{1,0:T(2,128)(2,1)S(1)} %bitcast.141), channel_id=1, source_target_pairs={{1,0},{2,1},{3,2},{4,3},{5,4},{6,5},{7,6},{8,7},{9,8},{10,9},{11,1... | collective-permute-start | bytes 3080 | tf_op jit(solution)/shard_map/ppermute | solution.py:23
  84.3 18.6 %collective-permute-start.8 = (bf16[1,512]{1,0:T(2,128)(2,1)S(1)}, bf16[1,512]{1,0:T(2,128)(2,1)S(1)}, u32[]{:S(2)}, u32[]{:S(2)}) collective-permute-start(bf16[1,512]{1,0:T(2,128)(2,1)S(1)} %bitcast.140), channel_id=1, source_target_pairs={{127,0},{0,1},{1,2},{2,3},{3,4},{4,5},{5,6},{6,7},{7,8},{8,9},{9,1... | collective-permute-start | bytes 3080 | tf_op jit(solution)/shard_map/ppermute | solution.py:23
  90.7 36.6 %all-to-all-start.1 = ((bf16[128,2,512]{2,1,0:T(2,128)(2,1)}), bf16[128,2,512]{2,1,0:T(2,128)(2,1)S(1)}, u32[]{:S(2)}, u32[]{:S(2)}) async-start(bf16[128,2,512]{2,1,0:T(2,128)(2,1)} %scatter_fusion.1), calls=%async_computation.1 | async-start | bytes 524288 | tf_op jit(solution)/shard_map/all_to_all | solution.py:158
  98.5 82.0 %all-reduce.3.cloned.1.call-start = ((), (), s32[]{:S(2)}) async-start(), calls=%async_computation.2 | async-start | bytes 131072 | tf_op jit(solution)/shard_map/psum | solution.py:241
  99.0 14.5 %collective-permute-start.4 = (bf16[1,128,128]{2,1,0:T(8,128)(2,1)S(1)}, bf16[1,128,128]{2,1,0:T(8,128)(2,1)S(1)}, u32[]{:S(2)}, u32[]{:S(2)}) collective-permute-start(bf16[1,128,128]{2,1,0:T(8,128)(2,1)S(1)} %bitcast.121), channel_id=1, source_target_pairs={{127,0},{0,1},{1,2},{2,3},{3,4},{4,5},{5,6},{6,7},{7,8},{8,9},{9,1... | collective-permute-start | bytes 98312 | tf_op jit(solution)/shard_map/ppermute | solution.py:23
  103.0 14.6 %collective-permute-start.7 = (bf16[1,128,128]{2,1,0:T(8,128)(2,1)S(1)}, bf16[1,128,128]{2,1,0:T(8,128)(2,1)S(1)}, u32[]{:S(2)}, u32[]{:S(2)}) collective-permute-start(bf16[1,128,128]{2,1,0:T(8,128)(2,1)S(1)} %bitcast.122), channel_id=1, source_target_pairs={{1,0},{2,1},{3,2},{4,3},{5,4},{6,5},{7,6},{8,7},{9,8},{10,9},{11,1... | collective-permute-start | bytes 98312 | tf_op jit(solution)/shard_map/ppermute | solution.py:23
  110.7 10.4 %collective-permute-start.6 = (bf16[1,128,128]{2,1,0:T(8,128)(2,1)S(1)}, bf16[1,128,128]{2,1,0:T(8,128)(2,1)S(1)}, u32[]{:S(2)}, u32[]{:S(2)}) collective-permute-start(bf16[1,128,128]{2,1,0:T(8,128)(2,1)S(1)} %bitcast.123), channel_id=1, source_target_pairs={{127,0},{0,1},{1,2},{2,3},{3,4},{4,5},{5,6},{6,7},{7,8},{8,9},{9,1... | collective-permute-start | bytes 98312 | tf_op jit(solution)/shard_map/ppermute | solution.py:23
  133.6 47.0 %copy-start.13 = (f32[512]{0:T(512)S(1)}, f32[512]{0:T(512)}, u32[]{:S(2)}) copy-start(f32[512]{0:T(512)} %param.35) | copy-start | bytes 6148
  134.3 48.4 %copy-start.20 = (f32[512]{0:T(512)S(1)}, f32[512]{0:T(512)}, u32[]{:S(2)}) copy-start(f32[512]{0:T(512)} %param.36) | copy-start | bytes 6148
  135.4 96.9 %all-reduce.5.cloned.1.call-start = ((), (), s32[]{:S(2)}) async-start(), calls=%async_computation.3 | async-start | bytes 131072 | tf_op jit(solution)/shard_map/psum | solution.py:252
  184.4 47.9 %copy-start.17 = (f32[512]{0:T(512)S(1)}, f32[512]{0:T(512)}, u32[]{:S(2)}) copy-start(f32[512]{0:T(512)} %param.39) | copy-start | bytes 6148
  185.3 50.1 %copy-start.18 = (f32[64]{0:T(128)S(1)}, f32[64]{0:T(128)}, u32[]{:S(2)}) copy-start(f32[64]{0:T(128)} %param.41) | copy-start | bytes 772
  191.7 44.0 %copy-start.4 = (bf16[32,128,128]{2,1,0:T(8,128)(2,1)}, bf16[32,128,128]{2,1,0:T(8,128)(2,1)S(1)}, u32[]{:S(2)}) copy-start(bf16[32,128,128]{2,1,0:T(8,128)(2,1)S(1)} %scatter_fusion.9) | copy-start | bytes 3145732
  193.8 41.9 %copy-start.3 = (bf16[32,128,128]{2,1,0:T(8,128)(2,1)}, bf16[32,128,128]{2,1,0:T(8,128)(2,1)S(1)}, u32[]{:S(2)}) copy-start(bf16[32,128,128]{2,1,0:T(8,128)(2,1)S(1)} %scatter_fusion.11) | copy-start | bytes 3145732
  (11 other events, 48.0 us)
Sparse Core Ops, SparseCore 0:
  135.5 45.0 all-reduce.2
  185.2 47.0 all-reduce.4
where the time goes:
time: 244 us
  waiting for transfers between devices  86.8 us (36%)
  starting transfers between devices  79.6 us (33%)
  local copies, waits for them, and re-layouts  42.6 us (17%)
  between operations  15 us (6%)
  other arithmetic  11.2 us (5%)
  matrix products  8.35 us (3%)
    ppermute x10, starting transfers between devices, passed_along(): return lax.ppermute(block, axis, route)  50.8 us
    psum x1, waiting for transfers between devices, local(): lax.psum(partial_heads.astype(jnp.bfloat16), 'section').astype(jnp.float32)  44.9 us
    psum x1, waiting for transfers between devices, local(): lax.psum(partial_units.astype(jnp.bfloat16), 'section').astype(jnp.float32)  38.3 us
    all_to_all x1, starting transfers between devices, local(): lax.all_to_all(send_codes, 'batch', split_axis=0, concat_axis=0, tiled=True)  20.8 us
    scatter x10, local copies, waits for them, and re-layouts, pack_side(): return tuple((jnp.zeros((MOVE,) + source_array.shape[1:], source_array.dt...  13.1 us
    all_to_all x1, starting transfers between devices, local(): lax.all_to_all(send_rows, 'batch', split_axis=0, concat_axis=0, tiled=True)  7.84 us
  transfers between devices with their start and end apart: 14, of which 3 were waited for; matrix products, arithmetic and copies ran while one was open for 17% of the time, Pallas kernels for 0%

commit v1 on v0

--- a/solution.py
+++ b/solution.py
@@ -1,3 +1,4 @@
+import functools
 import jax
 import jax.numpy as jnp
 from jax import lax
@@ -7,6 +8,14 @@
 MOVE = 1
 EPSILON = 1e-05
 MAX_PERIOD = 10000.0
+
+
+def handle_ranges(shard_in, axis_name):
+    upper = jnp.sum(lax.all_gather(shard_in, axis_name), 0)
+    return upper
+
+
+recover_row = functools.partial(handle_ranges, axis_name="section")
 
 
 def for_sending(array):
@@ -249,7 +258,7 @@
         jnp.dot(normed_two, in_weight, preferred_element_type=jnp.float32), approximate=False
     ).astype(jnp.bfloat16)
     partial_units = jnp.dot(inner_units, down_weight, preferred_element_type=jnp.float32)
-    feed_forward = lax.psum(partial_units.astype(jnp.bfloat16), "section").astype(jnp.float32)
+    feed_forward = recover_row(partial_units.astype(jnp.bfloat16)).astype(jnp.float32)
     residual_two = residual_one + scale_feedforward * feed_forward.reshape(streams, 2, model_width)
     excited = jax.nn.elu(residual_two).astype(jnp.bfloat16)
     earlier = jnp.stack([conv_prev, excited[:, 0]], axis=1)

time: 244 us -> 201 us (0.82)
  waiting for transfers between devices: 86.8 us -> 39.8 us
  blocking collectives: 0 us -> 5.86 us
    psum x1 -> x0, waiting for transfers between devices: 38.3 us -> none  [local(): lax.psum(partial_units.astype(jnp.bfloat16), 'section').astype(jnp.float32)]
    psum x1, waiting for transfers between devices: 44.9 us -> 36.2 us  [local(): lax.psum(partial_heads.astype(jnp.bfloat16), 'section').astype(jnp.float32)]
    all_gather x0 -> x1, blocking collectives: none -> 5.86 us  [handle_ranges(): upper = jnp.sum(lax.all_gather(shard_in, axis_name), 0)]
  transfers between devices with their start and end apart: 14 -> 13, of which waited for: 3 -> 2; matrix products, arithmetic and copies ran while one was open for 17% -> 21% of each run, Pallas kernels for 0% -> 0%
where the time goes in v1:
time: 201 us; the launch traced here: 200 us
  starting transfers between devices  79.5 us (40%)
  local copies, waits for them, and re-layouts  42.3 us (21%)
  waiting for transfers between devices  39.8 us (20%)
  between operations  15 us (7%)
  other arithmetic  10.3 us (5%)
  matrix products  7.34 us (4%)
  blocking collectives  5.86 us (3%)
    ppermute x10, starting transfers between devices, passed_along(): return lax.ppermute(block, axis, route)  50.8 us
    psum x1, waiting for transfers between devices, local(): lax.psum(partial_heads.astype(jnp.bfloat16), 'section').astype(jnp.float32)  36.2 us
    all_to_all x1, starting transfers between devices, local(): lax.all_to_all(send_codes, 'batch', split_axis=0, concat_axis=0, tiled=True)  20.8 us
    scatter x10, local copies, waits for them, and re-layouts, pack_side(): return tuple((jnp.zeros((MOVE,) + source_array.shape[1:], source_array.dt...  13.1 us
    all_to_all x1, starting transfers between devices, local(): lax.all_to_all(send_rows, 'batch', split_axis=0, concat_axis=0, tiled=True)  7.84 us
    all_gather x1, blocking collectives, handle_ranges(): upper = jnp.sum(lax.all_gather(shard_in, axis_name), 0)  5.86 us
    scatter x1, local copies, waits for them, and re-layouts, local(): send_rows = jnp.zeros((owners, capacity, model_width), jnp.bfloat16).at[t...  4.44 us
    scatter x2, local copies, waits for them, and re-layouts, local(): new_keys = keys_old.at[slot_ids, slot_first].set(fresh_keys[:, 0]).at[slo...  4.27 us
  transfers between devices with their start and end apart: 13, of which 2 were waited for; matrix products, arithmetic and copies ran while one was open for 21% of the time, Pallas kernels for 0%

profile of v1, /device:TPU:1, one launch (start us, length us, event | category | flops | bytes accessed | tf_op | source)
XLA Modules:
  0.0 200.1 jit_solution(1457648365820301183)
XLA Ops:
  8.1 2.0 %scatter_fusion = bf16[128,2]{0,1:T(2,128)(2,1)S(1)} fusion(bf16[128,2]{0,1:T(2,128)(2,1)S(1)} %broadcast_in_dim.63, s32[32]{0:T(128)S(1)} %fusion.115, bf16[32]{0:T(256)(128)(2,1)S(1)} %get-tuple-element.62), kind=kCustom, calls=%fused_computation.4 | custom fusion | bytes 448 | tf_op jit(solution)/shard_map/scatter | solution.py:164
  10.9 20.8 %all-to-all-start = ((bf16[128,1,2]{2,1,0:T(2,128)(2,1)}), bf16[128,1,2]{2,1,0:T(2,128)(2,1)S(1)}, u32[]{:S(2)}, u32[]{:S(2)}) async-start(bf16[128,1,2]{2,1,0:T(2,128)(2,1)} %copy.94), calls=%async_computation | async-start | bytes 131072 | tf_op jit(solution)/shard_map/all_to_all | solution.py:168
  32.7 9.0 %collective-permute-start.1 = (bf16[1,512]{1,0:T(2,128)(2,1)S(1)}, bf16[1,512]{1,0:T(2,128)(2,1)S(1)}, u32[]{:S(2)}, u32[]{:S(2)}) collective-permute-start(bf16[1,512]{1,0:T(2,128)(2,1)S(1)} %bitcast.140), channel_id=1, source_target_pairs={{1,0},{2,1},{3,2},{4,3},{5,4},{6,5},{7,6},{8,7},{9,8},{10,9},{11,1... | collective-permute-start | bytes 3080 | tf_op jit(solution)/shard_map/ppermute | solution.py:32
  42.5 1.9 collective-permute-start
  46.2 9.1 %collective-permute-start.3 = (bf16[1]{0:T(256)(128)(2,1)}, bf16[1]{0:T(256)(128)(2,1)}, u32[]{:S(2)}, u32[]{:S(2)}) collective-permute-start(bf16[1]{0:T(256)(128)(2,1)} %scatter_fusion.3), channel_id=1, source_target_pairs={{1,0},{2,1},{3,2},{4,3},{5,4},{6,5},{7,6},{8,7},{9,8},{10,9},{11,1... | collective-permute-start | bytes 14 | tf_op jit(solution)/shard_map/ppermute | solution.py:32
  57.0 1.9 collective-permute-start.2
  60.7 9.1 %collective-permute-start.5 = (bf16[1,128,128]{2,1,0:T(8,128)(2,1)S(1)}, bf16[1,128,128]{2,1,0:T(8,128)(2,1)S(1)}, u32[]{:S(2)}, u32[]{:S(2)}) collective-permute-start(bf16[1,128,128]{2,1,0:T(8,128)(2,1)S(1)} %bitcast.121), channel_id=1, source_target_pairs={{1,0},{2,1},{3,2},{4,3},{5,4},{6,5},{7,6},{8,7},{9,8},{10,9},{11,1... | collective-permute-start | bytes 98312 | tf_op jit(solution)/shard_map/ppermute | solution.py:32
  77.6 4.4 %scatter_fusion.1 = bf16[128,2,512]{2,1,0:T(2,128)(2,1)} fusion(bf16[128,2,512]{2,1,0:T(2,128)(2,1)} %broadcast_in_dim.65, s32[32]{0:T(128)S(1)} %fusion.115, bf16[32,512]{1,0:T(8,128)(2,1)S(1)} %copy-done.10), kind=kCustom, calls=%fused_computation.5 | custom fusion | bytes 98560 | tf_op jit(solution)/shard_map/scatter | solution.py:159
  82.4 1.9 collective-permute-start.9
  84.3 4.9 %collective-permute-start.8 = (bf16[1,512]{1,0:T(2,128)(2,1)S(1)}, bf16[1,512]{1,0:T(2,128)(2,1)S(1)}, u32[]{:S(2)}, u32[]{:S(2)}) collective-permute-start(bf16[1,512]{1,0:T(2,128)(2,1)S(1)} %bitcast.142), channel_id=1, source_target_pairs={{127,0},{0,1},{1,2},{2,3},{3,4},{4,5},{5,6},{6,7},{7,8},{8,9},{9,1... | collective-permute-start | bytes 3080 | tf_op jit(solution)/shard_map/ppermute | solution.py:32
  90.7 7.8 %all-to-all-start.1 = ((bf16[128,2,512]{2,1,0:T(2,128)(2,1)}), bf16[128,2,512]{2,1,0:T(2,128)(2,1)S(1)}, u32[]{:S(2)}, u32[]{:S(2)}) async-start(bf16[128,2,512]{2,1,0:T(2,128)(2,1)} %scatter_fusion.1), calls=%async_computation.1 | async-start | bytes 524288 | tf_op jit(solution)/shard_map/all_to_all | solution.py:167
  99.0 4.0 %collective-permute-start.4 = (bf16[1,128,128]{2,1,0:T(8,128)(2,1)S(1)}, bf16[1,128,128]{2,1,0:T(8,128)(2,1)S(1)}, u32[]{:S(2)}, u32[]{:S(2)}) collective-permute-start(bf16[1,128,128]{2,1,0:T(8,128)(2,1)S(1)} %bitcast.122), channel_id=1, source_target_pairs={{127,0},{0,1},{1,2},{2,3},{3,4},{4,5},{5,6},{6,7},{7,8},{8,9},{9,1... | collective-permute-start | bytes 98312 | tf_op jit(solution)/shard_map/ppermute | solution.py:32
  103.0 7.0 %collective-permute-start.7 = (bf16[1,128,128]{2,1,0:T(8,128)(2,1)S(1)}, bf16[1,128,128]{2,1,0:T(8,128)(2,1)S(1)}, u32[]{:S(2)}, u32[]{:S(2)}) collective-permute-start(bf16[1,128,128]{2,1,0:T(8,128)(2,1)S(1)} %bitcast.123), channel_id=1, source_target_pairs={{1,0},{2,1},{3,2},{4,3},{5,4},{6,5},{7,6},{8,7},{9,8},{10,9},{11,1... | collective-permute-start | bytes 98312 | tf_op jit(solution)/shard_map/ppermute | solution.py:32
  110.7 2.1 %collective-permute-start.6 = (bf16[1,128,128]{2,1,0:T(8,128)(2,1)S(1)}, bf16[1,128,128]{2,1,0:T(8,128)(2,1)S(1)}, u32[]{:S(2)}, u32[]{:S(2)}) collective-permute-start(bf16[1,128,128]{2,1,0:T(8,128)(2,1)S(1)} %bitcast.124), channel_id=1, source_target_pairs={{127,0},{0,1},{1,2},{2,3},{3,4},{4,5},{5,6},{6,7},{7,8},{8,9},{9,1... | collective-permute-start | bytes 98312 | tf_op jit(solution)/shard_map/ppermute | solution.py:32
  114.7 2.9 %gather_fusion.1 = bf16[32,128,128]{2,1,0:T(8,128)(2,1)} fusion(bf16[34,128,128]{2,1,0:T(8,128)(2,1)} %pad_maximum_fusion, s32[1024]{0:T(1024)S(1)} %pad_clamp_fusion), kind=kCustom, calls=%fused_computation.1.clone | custom fusion | bytes 2097280 | tf_op jit(solution)/shard_map/jit(_take)/gather | solution.py:217
  117.6 3.6 %collective-permute-done.6 = bf16[1,128,128]{2,1,0:T(8,128)(2,1)S(1)} collective-permute-done((bf16[1,128,128]{2,1,0:T(8,128)(2,1)S(1)}, bf16[1,128,128]{2,1,0:T(8,128)(2,1)S(1)}, u32[]{:S(2)}, u32[]{:S(2)}) %collective-permute-start.6) | collective-permute-done | bytes 32800 | tf_op jit(solution)/shard_map/ppermute | solution.py:32
  122.9 1.8 broadcast_select_fusion.1
  135.8 2.1 %scatter_fusion.8 = bf16[32,128,128]{2,1,0:T(8,128)(2,1)S(1)} fusion(bf16[32,128,128]{2,1,0:T(8,128)(2,1)S(1)} %get-tuple-element.57, s32[32]{0:T(128)S(1)} %get-tuple-element.55, bf16[32,128]{1,0:T(8,128)(2,1)S(1)} %copy.113), kind=kCustom, calls=%fused_computation.16 | custom fusion | bytes 24832 | tf_op jit(solution)/shard_map/scatter | solution.py:278
  138.0 2.1 %scatter_fusion.10 = bf16[32,128,128]{2,1,0:T(8,128)(2,1)S(1)} fusion(bf16[32,128,128]{2,1,0:T(8,128)(2,1)S(1)} %get-tuple-element.56, s32[32]{0:T(128)S(1)} %get-tuple-element.55, bf16[32,128]{1,0:T(8,128)(2,1)S(1)} %get-tuple-element.47), kind=kCustom, calls=%fused_computation.18 | custom fusion | bytes 24832 | tf_op jit(solution)/shard_map/scatter | solution.py:284
  140.1 2.1 %scatter_fusion.9 = bf16[32,128,128]{2,1,0:T(8,128)(2,1)S(1)} fusion(bf16[32,128,128]{2,1,0:T(8,128)(2,1)S(1)} %scatter_fusion.8, s32[32]{0:T(128)S(1)} %get-tuple-element.54, bf16[32,128]{1,0:T(8,128)(2,1)S(1)} %copy.114), kind=kCustom, calls=%fused_computation.17 | custom fusion | bytes 24832 | tf_op jit(solution)/shard_map/scatter | solution.py:280
  142.3 2.1 %scatter_fusion.11 = bf16[32,128,128]{2,1,0:T(8,128)(2,1)S(1)} fusion(bf16[32,128,128]{2,1,0:T(8,128)(2,1)S(1)} %scatter_fusion.10, s32[32]{0:T(128)S(1)} %get-tuple-element.54, bf16[32,128]{1,0:T(8,128)(2,1)S(1)} %get-tuple-element.46), kind=kCustom, calls=%fused_computation.19 | custom fusion | bytes 24832 | tf_op jit(solution)/shard_map/scatter | solution.py:286
  144.4 36.2 %all-reduce.2.cloned.1.call-done = bf16[64,512]{1,0:T(8,128)(2,1)} async-done(((bf16[64,512]{1,0:T(8,128)(2,1)}), bf16[64,512]{1,0:T(8,128)(2,1)}) %all-reduce.2.cloned.1.call-update) | async-done | bytes 65552 | tf_op jit(solution)/shard_map/psum | solution.py:250
  182.7 1.8 convolution_convert_fusion
  184.5 5.9 %all-gather = bf16[256,512]{1,0:T(8,128)(2,1)S(1)} all-gather(bf16[64,512]{1,0:T(8,128)(2,1)S(1)} %convolution_convert_fusion), channel_id=2, replica_groups=mesh['section'=4,'batch'=128] {'section'}, dimensions={0}, use_global_device_ids=true | all-gather | bytes 327680 | tf_op jit(solution)/shard_map/all_gather | solution.py:14
  (162 shorter events, 38.6 us)
Async XLA Ops:
  7.2 175.5 %copy-start = (bf16[512,512]{1,0:T(8,128)(2,1)S(1)}, bf16[512,512]{1,0:T(8,128)(2,1)}, u32[]{:S(2)}) copy-start(bf16[512,512]{1,0:T(8,128)(2,1)} %param.38) | copy-start | bytes 1572868
  7.2 24.6 %copy-start.19 = (s32[32]{0:T(128)S(1)}, s32[32]{0:T(128)}, u32[]{:S(2)}) copy-start(s32[32]{0:T(128)} %param.29) | copy-start | bytes 388
  7.2 24.8 %copy-start.12 = (bf16[32,512]{1,0:T(8,128)(2,1)S(1)}, bf16[32,512]{1,0:T(8,128)(2,1)}, u32[]{:S(2)}) copy-start(bf16[32,512]{1,0:T(8,128)(2,1)} %param.27) | copy-start | bytes 98308
  10.9 79.8 %all-to-all-start = ((bf16[128,1,2]{2,1,0:T(2,128)(2,1)}), bf16[128,1,2]{2,1,0:T(2,128)(2,1)S(1)}, u32[]{:S(2)}, u32[]{:S(2)}) async-start(bf16[128,1,2]{2,1,0:T(2,128)(2,1)} %copy.94), calls=%async_computation | async-start | bytes 131072 | tf_op jit(solution)/shard_map/all_to_all | solution.py:168
  31.8 27.2 %copy-start.1 = (bf16[32,128,128]{2,1,0:T(8,128)(2,1)S(1)}, bf16[32,128,128]{2,1,0:T(8,128)(2,1)}, u32[]{:S(2)}) copy-start(bf16[32,128,128]{2,1,0:T(8,128)(2,1)} %param.26) | copy-start | bytes 3145732
  32.7 78.1 %collective-permute-start.1 = (bf16[1,512]{1,0:T(2,128)(2,1)S(1)}, bf16[1,512]{1,0:T(2,128)(2,1)S(1)}, u32[]{:S(2)}, u32[]{:S(2)}) collective-permute-start(bf16[1,512]{1,0:T(2,128)(2,1)S(1)} %bitcast.140), channel_id=1, source_target_pairs={{1,0},{2,1},{3,2},{4,3},{5,4},{6,5},{7,6},{8,7},{9,8},{10,9},{11,1... | collective-permute-start | bytes 3080 | tf_op jit(solution)/shard_map/ppermute | solution.py:32
  42.5 70.4 %collective-permute-start = (bf16[1,512]{1,0:T(2,128)(2,1)S(1)}, bf16[1,512]{1,0:T(2,128)(2,1)S(1)}, u32[]{:S(2)}, u32[]{:S(2)}) collective-permute-start(bf16[1,512]{1,0:T(2,128)(2,1)S(1)} %bitcast.141), channel_id=1, source_target_pairs={{127,0},{0,1},{1,2},{2,3},{3,4},{4,5},{5,6},{6,7},{7,8},{8,9},{9,1... | collective-permute-start | bytes 3080 | tf_op jit(solution)/shard_map/ppermute | solution.py:32
  46.2 38.1 %collective-permute-start.3 = (bf16[1]{0:T(256)(128)(2,1)}, bf16[1]{0:T(256)(128)(2,1)}, u32[]{:S(2)}, u32[]{:S(2)}) collective-permute-start(bf16[1]{0:T(256)(128)(2,1)} %scatter_fusion.3), channel_id=1, source_target_pairs={{1,0},{2,1},{3,2},{4,3},{5,4},{6,5},{7,6},{8,7},{9,8},{10,9},{11,1... | collective-permute-start | bytes 14 | tf_op jit(solution)/shard_map/ppermute | solution.py:32
  57.0 25.4 %collective-permute-start.2 = (bf16[1]{0:T(256)(128)(2,1)}, bf16[1]{0:T(256)(128)(2,1)}, u32[]{:S(2)}, u32[]{:S(2)}) collective-permute-start(bf16[1]{0:T(256)(128)(2,1)} %scatter_fusion.2), channel_id=1, source_target_pairs={{127,0},{0,1},{1,2},{2,3},{3,4},{4,5},{5,6},{6,7},{7,8},{8,9},{9,1... | collective-permute-start | bytes 14 | tf_op jit(solution)/shard_map/ppermute | solution.py:32
  59.0 10.8 %copy-start.15 = (s32[32]{0:T(128)S(1)}, s32[32]{0:T(128)}, u32[]{:S(2)}) copy-start(s32[32]{0:T(128)} %param.30) | copy-start | bytes 388
  59.0 11.1 %copy-start.14 = (f32[4,512]{1,0:T(4,128)S(1)}, f32[4,512]{1,0:T(4,128)}, u32[]{:S(2)}) copy-start(f32[4,512]{1,0:T(4,128)} %param.31) | copy-start | bytes 24580
  60.7 52.8 %collective-permute-start.5 = (bf16[1,128,128]{2,1,0:T(8,128)(2,1)S(1)}, bf16[1,128,128]{2,1,0:T(8,128)(2,1)S(1)}, u32[]{:S(2)}, u32[]{:S(2)}) collective-permute-start(bf16[1,128,128]{2,1,0:T(8,128)(2,1)S(1)} %bitcast.121), channel_id=1, source_target_pairs={{1,0},{2,1},{3,2},{4,3},{5,4},{6,5},{7,6},{8,7},{9,8},{10,9},{11,1... | collective-permute-start | bytes 98312 | tf_op jit(solution)/shard_map/ppermute | solution.py:32
  82.4 16.6 %collective-permute-start.9 = (bf16[1,512]{1,0:T(2,128)(2,1)S(1)}, bf16[1,512]{1,0:T(2,128)(2,1)S(1)}, u32[]{:S(2)}, u32[]{:S(2)}) collective-permute-start(bf16[1,512]{1,0:T(2,128)(2,1)S(1)} %bitcast.143), channel_id=1, source_target_pairs={{1,0},{2,1},{3,2},{4,3},{5,4},{6,5},{7,6},{8,7},{9,8},{10,9},{11,1... | collective-permute-start | bytes 3080 | tf_op jit(solution)/shard_map/ppermute | solution.py:32
  84.3 18.6 %collective-permute-start.8 = (bf16[1,512]{1,0:T(2,128)(2,1)S(1)}, bf16[1,512]{1,0:T(2,128)(2,1)S(1)}, u32[]{:S(2)}, u32[]{:S(2)}) collective-permute-start(bf16[1,512]{1,0:T(2,128)(2,1)S(1)} %bitcast.142), channel_id=1, source_target_pairs={{127,0},{0,1},{1,2},{2,3},{3,4},{4,5},{5,6},{6,7},{7,8},{8,9},{9,1... | collective-permute-start | bytes 3080 | tf_op jit(solution)/shard_map/ppermute | solution.py:32
  90.7 36.6 %all-to-all-start.1 = ((bf16[128,2,512]{2,1,0:T(2,128)(2,1)}), bf16[128,2,512]{2,1,0:T(2,128)(2,1)S(1)}, u32[]{:S(2)}, u32[]{:S(2)}) async-start(bf16[128,2,512]{2,1,0:T(2,128)(2,1)} %scatter_fusion.1), calls=%async_computation.1 | async-start | bytes 524288 | tf_op jit(solution)/shard_map/all_to_all | solution.py:167
  98.5 82.1 %all-reduce.2.cloned.1.call-start = ((), (), s32[]{:S(2)}) async-start(), calls=%async_computation.2 | async-start | bytes 131072 | tf_op jit(solution)/shard_map/psum | solution.py:250
  99.0 14.5 %collective-permute-start.4 = (bf16[1,128,128]{2,1,0:T(8,128)(2,1)S(1)}, bf16[1,128,128]{2,1,0:T(8,128)(2,1)S(1)}, u32[]{:S(2)}, u32[]{:S(2)}) collective-permute-start(bf16[1,128,128]{2,1,0:T(8,128)(2,1)S(1)} %bitcast.122), channel_id=1, source_target_pairs={{127,0},{0,1},{1,2},{2,3},{3,4},{4,5},{5,6},{6,7},{7,8},{8,9},{9,1... | collective-permute-start | bytes 98312 | tf_op jit(solution)/shard_map/ppermute | solution.py:32
  103.0 14.6 %collective-permute-start.7 = (bf16[1,128,128]{2,1,0:T(8,128)(2,1)S(1)}, bf16[1,128,128]{2,1,0:T(8,128)(2,1)S(1)}, u32[]{:S(2)}, u32[]{:S(2)}) collective-permute-start(bf16[1,128,128]{2,1,0:T(8,128)(2,1)S(1)} %bitcast.123), channel_id=1, source_target_pairs={{1,0},{2,1},{3,2},{4,3},{5,4},{6,5},{7,6},{8,7},{9,8},{10,9},{11,1... | collective-permute-start | bytes 98312 | tf_op jit(solution)/shard_map/ppermute | solution.py:32
  110.7 10.4 %collective-permute-start.6 = (bf16[1,128,128]{2,1,0:T(8,128)(2,1)S(1)}, bf16[1,128,128]{2,1,0:T(8,128)(2,1)S(1)}, u32[]{:S(2)}, u32[]{:S(2)}) collective-permute-start(bf16[1,128,128]{2,1,0:T(8,128)(2,1)S(1)} %bitcast.124), channel_id=1, source_target_pairs={{127,0},{0,1},{1,2},{2,3},{3,4},{4,5},{5,6},{6,7},{7,8},{8,9},{9,1... | collective-permute-start | bytes 98312 | tf_op jit(solution)/shard_map/ppermute | solution.py:32
  134.3 46.3 %copy-start.13 = (f32[512]{0:T(512)S(1)}, f32[512]{0:T(512)}, u32[]{:S(2)}) copy-start(f32[512]{0:T(512)} %param.35) | copy-start | bytes 6148
  134.5 48.2 %copy-start.20 = (f32[512]{0:T(512)S(1)}, f32[512]{0:T(512)}, u32[]{:S(2)}) copy-start(f32[512]{0:T(512)} %param.36) | copy-start | bytes 6148
  142.2 42.2 %copy-start.4 = (bf16[32,128,128]{2,1,0:T(8,128)(2,1)}, bf16[32,128,128]{2,1,0:T(8,128)(2,1)S(1)}, u32[]{:S(2)}) copy-start(bf16[32,128,128]{2,1,0:T(8,128)(2,1)S(1)} %scatter_fusion.9) | copy-start | bytes 3145732
  144.4 40.1 %copy-start.3 = (bf16[32,128,128]{2,1,0:T(8,128)(2,1)}, bf16[32,128,128]{2,1,0:T(8,128)(2,1)S(1)}, u32[]{:S(2)}) copy-start(bf16[32,128,128]{2,1,0:T(8,128)(2,1)S(1)} %scatter_fusion.11) | copy-start | bytes 3145732
  182.7 7.9 %copy-start.17 = (f32[512]{0:T(512)S(1)}, f32[512]{0:T(512)}, u32[]{:S(2)}) copy-start(f32[512]{0:T(512)} %param.39) | copy-start | bytes 6148
  (10 other events, 24.1 us)
Sparse Core Ops, SparseCore 0:
  135.6 45.0 all-reduce.1
